TPU v7x, 256 devices: a whole 4x4x8 slice. The times are simulated.
256 devices in a mesh: dp: 32 (over x, z_hi, core), tensor: 8 (over y, z_lo).
Axes of the slice: x: 4, y: 4, z: 8 (z_hi: 4, z_lo: 2; z = z_hi * 2 + z_lo), core: 2. Of those that a mesh axis runs over, the one named last changes fastest.
Arguments:
- stream: bfloat16 [64, 430, 2048], P('dp', None, 'tensor'), may hold values from -3 to 3
- normed: bfloat16 [64, 430, 2048], P('dp'), may hold values from -6 to 6
- query_weight: bfloat16 [2048, 2048], P(None, 'tensor'), as said below
- key_weight: bfloat16 [2048, 2048], P(None, 'tensor'), as said below
- value_weight: bfloat16 [2048, 2048], P(None, 'tensor'), may hold values from -0.125 to 0.125
- out_weight: bfloat16 [2048, 2048], P('tensor'), may hold values from -0.125 to 0.125
- norm_gain: bfloat16 [2048], P('tensor'), may hold values from 0.099609375 to 1.8984375
- proj_weight: bfloat16 [2048, 1024], P('tensor'), may hold values from -0.125 to 0.125
- images: bfloat16 [64, 1024], P('dp'), may hold values from -6 to 6
Outputs:
- mean_loss: float32 [], replicated
- grad_normed: bfloat16 [64, 430, 2048], P('dp', None, 'tensor')
- grad_query: float32 [2048, 2048], P('dp', 'tensor')
- grad_key: float32 [2048, 2048], P('dp', 'tensor')
- grad_value: float32 [2048, 2048], P('dp', 'tensor')
- grad_out: float32 [2048, 2048], P('tensor', 'dp')
- grad_proj: float32 [2048, 1024], P('tensor', 'dp')
Inputs may be any that keep to these rules, and one draw needn't show every extreme that they name: `query_weight`: query projection entries, independent draws of order 2048^-0.5. `key_weight`: key projection entries, of order 2048^-0.5, in some heads up to about sixteen times that, possibly aligned with the query projection.
All inputs are finite; a program needn't handle non-finite values.
Results may differ from a plain program's by a relative error of at most 0.02.
Values may be sent and summed in bfloat16 or wider, within the bound.
No kernel may reach another device: no remote copies, remote signals or barrier semaphores. Data moves between devices by JAX's collectives and lax.ppermute only.
A program may use at most 128 MiB of HBM per device.

v0:
```python
import jax
import jax.numpy as jnp
from jax import lax
from jax.sharding import PartitionSpec as P

D = 2048
H = 16


SCALE_LOGIT = 14.0
GRAD_SCALE = 256.0
EPSILON = 1e-05
HIGH = lax.Precision.HIGHEST


def project(inputs, weight):
    return jnp.einsum("bld,dc->blc", inputs, weight, preferred_element_type=jnp.float32).astype(
        jnp.bfloat16
    )


def split_heads(values, head_size):
    return values.reshape(values.shape[0], values.shape[1], values.shape[2] // head_size, head_size)


def local(
    stream,
    normed,
    query_weight,
    key_weight,
    value_weight,
    out_weight,
    norm_gain,
    proj_weight,
    images,
):
    seq_count = normed.shape[0]
    length = normed.shape[1]
    col_count = query_weight.shape[1]
    feat_share = stream.shape[2]
    head_size = D // H
    scale_head = head_size ** (-0.5)
    queries = split_heads(project(normed, query_weight), head_size)
    keys_all = split_heads(project(normed, key_weight), head_size)
    values_all = split_heads(project(normed, value_weight), head_size)
    scores = (
        jnp.einsum("bqhd,bkhd->bhqk", queries, keys_all, preferred_element_type=jnp.float32)
        * scale_head
    )
    row_max = jnp.max(scores, axis=-1, keepdims=True)
    exp_scores = jnp.exp(scores - row_max)
    attn_prob = exp_scores / jnp.sum(exp_scores, axis=-1, keepdims=True)
    attn_half = attn_prob.astype(jnp.bfloat16)
    heads_out = jnp.einsum(
        "bhqk,bkhd->bqhd", attn_half, values_all, preferred_element_type=jnp.float32
    )
    head_concat = heads_out.astype(jnp.bfloat16).reshape(seq_count, length, col_count)
    partial_value = jnp.einsum(
        "blc,cd->bld", head_concat, out_weight, preferred_element_type=jnp.float32
    )
    summed = lax.psum(partial_value.astype(jnp.bfloat16), "tensor").astype(jnp.float32)
    attended = lax.dynamic_slice_in_dim(
        summed, lax.axis_index("tensor") * feat_share, feat_share, 2
    )
    residual = stream.astype(jnp.float32) + attended
    center = lax.psum(jnp.sum(residual, axis=-1), "tensor") / D
    offset = residual - center[..., None]
    variance = lax.psum(jnp.sum(offset * offset, axis=-1), "tensor") / D
    inv_std = lax.rsqrt(variance + EPSILON)[..., None]
    normal_feat = (residual - center[..., None]) * inv_std
    gain_float = norm_gain.astype(jnp.float32)
    pooled = jnp.mean(normal_feat * gain_float, axis=1).astype(jnp.bfloat16)
    embedded = lax.psum(jnp.dot(pooled, proj_weight, preferred_element_type=jnp.float32), "tensor")
    embed_norm = jnp.sqrt(jnp.sum(embedded * embedded, axis=-1, keepdims=True) + EPSILON)
    spectra = embedded / embed_norm
    gathered = lax.all_gather(images, "dp", axis=0, tiled=True).astype(jnp.float32)
    image_unit = gathered / jnp.sqrt(jnp.sum(gathered * gathered, axis=-1, keepdims=True) + EPSILON)
    logits = SCALE_LOGIT * jnp.dot(spectra, image_unit.T, precision=HIGH)
    own_start = lax.axis_index("dp") * seq_count
    columns = jnp.arange(logits.shape[1], dtype=jnp.int32)
    own_rows = own_start + jnp.arange(seq_count, dtype=jnp.int32)
    matches = (columns[None, :] == own_rows[:, None]).astype(jnp.float32)
    exp_logits = jnp.exp(logits)
    row_lse = jnp.log(jnp.sum(exp_logits, axis=1))
    diagonal = jnp.sum(logits * matches, axis=1)
    local_loss = 0.5 * jnp.sum(row_lse) - jnp.sum(diagonal)
    col_total, loss_sum = lax.psum((jnp.sum(exp_logits, axis=0), local_loss), "dp")
    col_lse = jnp.log(col_total)
    mean_loss = (loss_sum + 0.5 * jnp.sum(col_lse)) / logits.shape[1]
    grad_logits = GRAD_SCALE * (
        0.5 * jnp.exp(logits - row_lse[:, None])
        + 0.5 * jnp.exp(logits - col_lse[None, :])
        - matches
    )
    grad_spec = SCALE_LOGIT * jnp.dot(grad_logits, image_unit, precision=HIGH)
    radial = jnp.sum(spectra * grad_spec, axis=-1, keepdims=True)
    grad_embed = ((grad_spec - spectra * radial) / embed_norm).astype(jnp.bfloat16)
    grad_proj = lax.dot_general(
        pooled, grad_embed, (((0,), (0,)), ((), ())), preferred_element_type=jnp.float32
    )
    grad_pooled = lax.dot_general(
        grad_embed, proj_weight, (((1,), (1,)), ((), ())), preferred_element_type=jnp.float32
    )
    grad_normal = jnp.broadcast_to(grad_pooled[:, None, :] / length, normal_feat.shape) * gain_float
    mean_one, mean_two = lax.psum(
        (jnp.sum(grad_normal, axis=-1), jnp.sum(grad_normal * normal_feat, axis=-1)), "tensor"
    )
    grad_resid = (
        inv_std * (grad_normal - mean_one[..., None] / D - normal_feat * (mean_two[..., None] / D))
    ).astype(jnp.bfloat16)
    piece_rows = lax.all_gather(grad_resid, "tensor", axis=2, tiled=True)
    grad_heads = jnp.einsum(
        "blw,cw->blc", piece_rows, out_weight, preferred_element_type=jnp.float32
    )
    update = jnp.einsum("blc,blw->cw", head_concat, piece_rows, preferred_element_type=jnp.float32)
    grad_out = update
    grad_heads, grad_out = (grad_heads, grad_out)
    grad_heads = split_heads(grad_heads.astype(jnp.bfloat16), head_size)
    grad_probs = jnp.einsum(
        "bqhd,bkhd->bhqk", grad_heads, values_all, preferred_element_type=jnp.float32
    )
    row_dot = jnp.sum(attn_prob * grad_probs, axis=-1, keepdims=True)
    grad_scores = (attn_prob * (grad_probs - row_dot) * scale_head).astype(jnp.bfloat16)
    grad_q = (
        jnp.einsum("bhqk,bkhd->bqhd", grad_scores, keys_all, preferred_element_type=jnp.float32)
        .astype(jnp.bfloat16)
        .reshape(seq_count, length, col_count)
    )
    grad_k = (
        jnp.einsum("bhqk,bqhd->bkhd", grad_scores, queries, preferred_element_type=jnp.float32)
        .astype(jnp.bfloat16)
        .reshape(seq_count, length, col_count)
    )
    grad_v = (
        jnp.einsum("bhqk,bqhd->bkhd", attn_half, grad_heads, preferred_element_type=jnp.float32)
        .astype(jnp.bfloat16)
        .reshape(seq_count, length, col_count)
    )
    back_input = jnp.einsum("blc,dc->bld", grad_q, query_weight, preferred_element_type=jnp.float32)
    back_input = back_input + jnp.einsum(
        "blc,dc->bld", grad_k, key_weight, preferred_element_type=jnp.float32
    )
    back_input = back_input + jnp.einsum(
        "blc,dc->bld", grad_v, value_weight, preferred_element_type=jnp.float32
    )
    grad_normed = lax.psum_scatter(
        back_input.astype(jnp.bfloat16), "tensor", scatter_dimension=2, tiled=True
    )
    grad_query = jnp.einsum("bld,blc->dc", normed, grad_q, preferred_element_type=jnp.float32)
    grad_key = jnp.einsum("bld,blc->dc", normed, grad_k, preferred_element_type=jnp.float32)
    grad_value = jnp.einsum("bld,blc->dc", normed, grad_v, preferred_element_type=jnp.float32)
    reduced = (
        lax.psum_scatter(
            grad_query.astype(jnp.bfloat16), "dp", scatter_dimension=0, tiled=True
        ).astype(jnp.float32),
        lax.psum_scatter(
            grad_key.astype(jnp.bfloat16), "dp", scatter_dimension=0, tiled=True
        ).astype(jnp.float32),
        lax.psum_scatter(
            grad_value.astype(jnp.bfloat16), "dp", scatter_dimension=0, tiled=True
        ).astype(jnp.float32),
        lax.psum_scatter(
            grad_out.astype(jnp.bfloat16), "dp", scatter_dimension=1, tiled=True
        ).astype(jnp.float32),
        lax.psum_scatter(
            grad_proj.astype(jnp.bfloat16), "dp", scatter_dimension=1, tiled=True
        ).astype(jnp.float32),
    )
    return (mean_loss, grad_normed, reduced[0], reduced[1], reduced[2], reduced[3], reduced[4])


def solution(mesh):
    return jax.shard_map(
        local,
        mesh=mesh,
        in_specs=(
            P("dp", None, "tensor"),
            P("dp", None, None),
            P(None, "tensor"),
            P(None, "tensor"),
            P(None, "tensor"),
            P("tensor", None),
            P("tensor"),
            P("tensor", None),
            P("dp", None),
        ),
        out_specs=(
            P(),
            P("dp", None, "tensor"),
            P("dp", "tensor"),
            P("dp", "tensor"),
            P("dp", "tensor"),
            P("tensor", "dp"),
            P("tensor", "dp"),
        ),
        check_vma=False,
    )
```

profile of v0, /device:TPU:1, one launch (start us, length us, event | category | flops | bytes accessed | tf_op | source)
XLA Modules:
  0.0 972.7 jit_solution(16875496119188521870)
XLA Ops:
  7.2 4.5 fusion.42
  11.9 4.0 fusion.45
  16.0 4.3 fusion.39
  21.2 2.8 fusion.122
  24.0 4.7 fusion.48
  29.4 3.0 convolution_convert_fusion
  32.5 50.5 %all-gather = bf16[32,2,1024]{2,1,0:T(2,128)(2,1)S(1)} all-gather(bf16[1,2,1024]{2,1,0:T(2,128)(2,1)S(1)} %bitcast.72), channel_id=1, replica_groups=mesh['dp'=32,'tensor'=8] {'dp'}, dimensions={0}, use_global_device_ids=true | all-gather | bytes 135168 | tf_op jit(solution)/shard_map/all_gather | solution.py:76
  83.2 117.2 %all-reduce.4.cloned.1.call-done = bf16[2,430,2048]{2,1,0:T(8,128)(2,1)} async-done(((bf16[2,430,2048]{2,1,0:T(8,128)(2,1)}), bf16[2,430,2048]{2,1,0:T(8,128)(2,1)}) %all-reduce.4.cloned.1.call-update) | async-done | bytes 3522576 | tf_op jit(solution)/shard_map/psum | solution.py:61
  200.4 1.2 fusion.73
  201.6 12.8 %psum.57 = f32[2,430]{1,0:T(2,128)S(1)} all-reduce(f32[2,430]{1,0:T(2,128)S(1)} %fusion.73), channel_id=1, replica_groups=mesh['dp'=32,'tensor'=8] {'tensor'}, use_global_device_ids=true, to_apply=%region_4.0 | all-reduce | flops 860 | bytes 6880 | tf_op jit(solution)/shard_map/psum | solution.py:66
  214.4 1.4 multiply_reduce_fusion.4
  215.8 13.8 %psum.58 = f32[2,430]{1,0:T(2,128)S(1)} all-reduce(f32[2,430]{1,0:T(2,128)S(1)} %multiply_reduce_fusion.4), channel_id=1, replica_groups=mesh['dp'=32,'tensor'=8] {'tensor'}, use_global_device_ids=true, to_apply=%region_6.0 | all-reduce | flops 860 | bytes 6880 | tf_op jit(solution)/shard_map/psum | solution.py:68
  229.7 1.3 multiply_reduce_fusion.3
  231.2 13.3 %psum.59 = f32[2,1024]{1,0:T(2,128)S(1)} all-reduce(f32[2,1024]{1,0:T(2,128)S(1)} %fusion.102), channel_id=1, replica_groups=mesh['dp'=32,'tensor'=8] {'tensor'}, use_global_device_ids=true, to_apply=%region_8.0 | all-reduce | flops 2048 | bytes 16384 | tf_op jit(solution)/shard_map/psum | solution.py:73
  244.6 1.0 exponential_reduce_fusion
  247.5 83.0 %all-reduce = (f32[64]{0:T(128)S(1)}, f32[]{:T(128)}) all-reduce(f32[64]{0:T(128)S(1)} %get-tuple-element.30, f32[]{:T(128)S(6)} %sub.68), channel_id=1, replica_groups=mesh['dp'=32,'tensor'=8] {'dp'}, use_global_device_ids=true, to_apply=%region_16.0 | all-reduce | flops 65 | bytes 520 | tf_op jit(solution)/shard_map/psum | solution.py:87
  331.9 1.6 multiply_reduce_fusion.2
  333.5 13.0 %all-reduce.1 = (f32[2,430]{1,0:T(2,128)S(1)}, f32[2,430]{1,0:T(2,128)S(1)}) all-reduce(f32[2,430]{1,0:T(2,128)S(1)} %get-tuple-element.29, f32[2,430]{1,0:T(2,128)S(1)} %get-tuple-element.28), channel_id=1, replica_groups=mesh['dp'=32,'tensor'=8] {'tensor'}, use_global_device_ids=true, to_apply=%region_22.0 | all-reduce | flops 1720 | bytes 13760 | tf_op jit(solution)/shard_map/psum | solution.py:105
  346.5 2.3 fusion.68
  349.0 1.3 convolution_convert_fusion.1
  350.3 73.9 %all-gather.3.cloned.1.call-done = bf16[2,430,2048]{2,1,0:T(8,128)(2,1)} async-done(((bf16[2,430,256]{2,1,0:T(8,128)(2,1)}), bf16[2,430,2048]{2,1,0:T(8,128)(2,1)}) %all-gather.3.cloned.1.call-update) | async-done | bytes 3522576 | tf_op jit(solution)/shard_map/all_gather | solution.py:111
  424.2 3.1 convolution_convert_fusion.3
  427.5 4.5 fusion.49
  432.6 4.4 fusion.12
  437.1 1.3 copy.93
  438.6 3.6 fusion.76
  442.2 6.6 fusion.50
  449.5 4.4 fusion.13
  453.9 1.3 copy.91
  455.3 7.0 fusion.53
  462.9 4.4 fusion.14
  467.4 1.3 copy.89
  468.8 4.9 fusion.11
  474.0 1.1 fusion.61
  475.2 1.1 fusion.58
  476.4 2.9 add_convert_fusion
  480.7 35.0 %reduce-scatter.17.cloned.1.call-done = bf16[256,32]{0,1:T(8,128)(2,1)} async-done(((bf16[256,1024]{0,1:T(8,128)(2,1)}), bf16[256,32]{0,1:T(8,128)(2,1)}) %reduce-scatter.17.cloned.1.call-update) | async-done | bytes 16400 | tf_op jit(solution)/shard_map/reduce_scatter | solution.py:165
  515.7 1.3 convert_element_type.147
  517.1 89.3 %reduce-scatter.23.cloned.1.call-done = bf16[64,256]{1,0:T(8,128)(2,1)} async-done(((bf16[2048,256]{1,0:T(8,128)(2,1)}), bf16[64,256]{1,0:T(8,128)(2,1)}) %reduce-scatter.23.cloned.1.call-update) | async-done | bytes 32784
  606.4 0.9 copy.94
  608.0 89.1 %reduce-scatter.21.cloned.1.call-done = bf16[64,256]{1,0:T(8,128)(2,1)} async-done(((bf16[2048,256]{1,0:T(8,128)(2,1)}), bf16[64,256]{1,0:T(8,128)(2,1)}) %reduce-scatter.21.cloned.1.call-update) | async-done | bytes 32784
  697.1 0.9 copy.92
  698.7 89.1 %reduce-scatter.19.cloned.1.call-done = bf16[64,256]{1,0:T(8,128)(2,1)} async-done(((bf16[2048,256]{1,0:T(8,128)(2,1)}), bf16[64,256]{1,0:T(8,128)(2,1)}) %reduce-scatter.19.cloned.1.call-update) | async-done | bytes 32784
  787.8 0.9 copy.90
  789.4 89.2 %reduce-scatter.15.cloned.1.call-done = bf16[256,64]{0,1:T(8,128)(2,1)} async-done(((bf16[256,2048]{0,1:T(8,128)(2,1)}), bf16[256,64]{0,1:T(8,128)(2,1)}) %reduce-scatter.15.cloned.1.call-update) | async-done | bytes 32784 | tf_op jit(solution)/shard_map/reduce_scatter | solution.py:162
  878.6 1.4 convert_element_type.145
  880.0 82.3 %reduce-scatter.13.cloned.1.call-done = bf16[2,430,256]{2,1,0:T(8,128)(2,1)} async-done(((bf16[2,430,2048]{2,1,0:T(8,128)(2,1)}), bf16[2,430,256]{2,1,0:T(8,128)(2,1)}) %reduce-scatter.13.cloned.1.call-update) | async-done | bytes 440336 | tf_op jit(solution)/shard_map/reduce_scatter | solution.py:146
  962.4 2.1 copy.83
  (73 shorter events, 9.3 us)
Async XLA Ops:
  7.2 22.2 %copy-start = (bf16[256,2048]{1,0:T(8,128)(2,1)S(1)}, bf16[256,2048]{1,0:T(8,128)(2,1)}, u32[]{:S(2)}) copy-start(bf16[256,2048]{1,0:T(8,128)(2,1)} %param.14) | copy-start | bytes 3145732
  7.2 4.7 copy-start.7
  7.2 193.2 %all-reduce.4.cloned.1.call-start = ((), (), s32[]{:S(2)}) async-start(), calls=%async_computation.6 | async-start | bytes 7077888 | tf_op jit(solution)/shard_map/psum | solution.py:61
  20.5 3.5 copy-start.3
  21.2 2.8 copy-start.1
  29.3 3.0 copy-start.5
  29.4 3.1 copy-start.12
  29.4 3.1 copy-start.11
  29.4 171.0 %copy-start.2 = (bf16[2,430,256]{2,0,1:T(2,128)(2,1)S(1)}, bf16[2,430,256]{2,0,1:T(2,128)(2,1)}, u32[]{:S(2)}) copy-start(bf16[2,430,256]{2,0,1:T(2,128)(2,1)} %param.9) | copy-start | bytes 1320964
  32.4 198.6 %copy-start.10 = (bf16[256,1024]{1,0:T(8,128)(2,1)S(1)}, bf16[256,1024]{1,0:T(8,128)(2,1)}, u32[]{:S(2)}) copy-start(bf16[256,1024]{1,0:T(8,128)(2,1)} %param.16) | copy-start | bytes 1572868
  32.4 391.8 %all-gather.3.cloned.1.call-start = ((), (), s32[]{:S(2)}) async-start(), calls=%async_computation.7 | async-start | bytes 3981312 | tf_op jit(solution)/shard_map/all_gather | solution.py:111
  348.9 166.8 %reduce-scatter.17.cloned.1.call-start = ((), (), s32[]{:S(2)}) async-start(), calls=%async_computation.10 | async-start | bytes 540672 | tf_op jit(solution)/shard_map/reduce_scatter | solution.py:165
  350.2 256.2 %reduce-scatter.23.cloned.1.call-start = ((), (), s32[]{:S(2)}) async-start(), calls=%async_computation.13 | async-start | bytes 1081344
  427.5 4.5 copy-start.4
  438.4 258.7 %reduce-scatter.21.cloned.1.call-start = ((), (), s32[]{:S(2)}) async-start(), calls=%async_computation.12 | async-start | bytes 1081344
  455.3 332.5 %reduce-scatter.19.cloned.1.call-start = ((), (), s32[]{:S(2)}) async-start(), calls=%async_computation.11 | async-start | bytes 1081344
  468.7 5.2 copy-start.6
  468.7 409.9 %reduce-scatter.15.cloned.1.call-start = ((), (), s32[]{:S(2)}) async-start(), calls=%async_computation.9 | async-start | bytes 1081344 | tf_op jit(solution)/shard_map/reduce_scatter | solution.py:162
  473.7 488.7 %reduce-scatter.13.cloned.1.call-start = ((), (), s32[]{:S(2)}) async-start(), calls=%async_computation.8 | async-start | bytes 3981312 | tf_op jit(solution)/shard_map/reduce_scatter | solution.py:146
  474.0 1.2 copy-start.8
  475.2 1.2 copy-start.9
Sparse Core Ops, SparseCore 0:
  32.5 167.8 all-reduce.3
  349.0 75.1 all-gather.2
  427.9 87.7 reduce-scatter.16
  519.4 86.9 reduce-scatter.22
  610.0 87.0 reduce-scatter.20
  700.7 87.0 reduce-scatter.18
  791.6 87.0 reduce-scatter.14
  881.2 81.0 reduce-scatter.12
where the time goes:
time: 982 us; the launch traced here: 973 us
  waiting for transfers between devices  665 us (68%)
  blocking collectives  186 us (19%)
  matrix products  72.4 us (7%)
  between operations  18.5 us (2%)
  other arithmetic  15 us (2%)
  local copies, waits for them, and re-layouts  14.2 us (1%)
    unnamed x11, waiting for transfers between devices  268 us
    psum x1, waiting for transfers between devices, local(): lax.psum(partial_value.astype(jnp.bfloat16), 'tensor').astype(jnp.float32)  117 us
    reduce_scatter x1, waiting for transfers between devices, local(): lax.psum_scatter(grad_out.astype(jnp.bfloat16), 'dp', scatter_dimension=1...  89.2 us
    psum x1, blocking collectives, local(): lax.psum((jnp.sum(exp_logits, axis=0), local_loss), 'dp')  83 us
    reduce_scatter x1, waiting for transfers between devices, local(): lax.psum_scatter(back_input.astype(jnp.bfloat16), 'tensor', scatter_dimen...  82.3 us
    all_gather x1, waiting for transfers between devices, local(): piece_rows = lax.all_gather(grad_resid, 'tensor', axis=2, tiled=True)  73.9 us
    all_gather x1, blocking collectives, local(): lax.all_gather(images, 'dp', axis=0, tiled=True).astype(jnp.float32)  50.5 us
    reduce_scatter x1, waiting for transfers between devices, local(): lax.psum_scatter(grad_proj.astype(jnp.bfloat16), 'dp', scatter_dimension=...  35 us
  transfers between devices with their start and end apart: 8, of which 8 were waited for; matrix products, arithmetic and copies ran while one was open for 6% of the time, Pallas kernels for 0%

commit v1 on v0

--- a/solution.py
+++ b/solution.py
@@ -21,6 +21,16 @@
 
 def split_heads(values, head_size):
     return values.reshape(values.shape[0], values.shape[1], values.shape[2] // head_size, head_size)
+
+
+def chunks_rows(grad, parts):
+    rows, cols = grad.shape
+    return grad.reshape(parts, (rows // parts) * cols)
+
+
+def chunks_cols(grad, parts):
+    rows, cols = grad.shape
+    return grad.reshape(rows, parts, cols // parts).transpose(1, 0, 2).reshape(parts, -1)
 
 
 def local(
@@ -40,6 +50,12 @@
     feat_share = stream.shape[2]
     head_size = D // H
     scale_head = head_size ** (-0.5)
+    dp_parts = lax.psum(1, "dp")
+    t_index = lax.axis_index("tensor")
+    gain_full = lax.all_gather(norm_gain, "tensor", axis=0, tiled=True).astype(jnp.float32)
+    gathered = lax.all_gather(images, "dp", axis=0, tiled=True).astype(jnp.float32)
+    image_unit = gathered / jnp.sqrt(jnp.sum(gathered * gathered, axis=-1, keepdims=True) + EPSILON)
+
     queries = split_heads(project(normed, query_weight), head_size)
     keys_all = split_heads(project(normed, key_weight), head_size)
     values_all = split_heads(project(normed, value_weight), head_size)
@@ -58,23 +74,27 @@
     partial_value = jnp.einsum(
         "blc,cd->bld", head_concat, out_weight, preferred_element_type=jnp.float32
     )
-    summed = lax.psum(partial_value.astype(jnp.bfloat16), "tensor").astype(jnp.float32)
-    attended = lax.dynamic_slice_in_dim(
-        summed, lax.axis_index("tensor") * feat_share, feat_share, 2
-    )
-    residual = stream.astype(jnp.float32) + attended
-    center = lax.psum(jnp.sum(residual, axis=-1), "tensor") / D
-    offset = residual - center[..., None]
-    variance = lax.psum(jnp.sum(offset * offset, axis=-1), "tensor") / D
-    inv_std = lax.rsqrt(variance + EPSILON)[..., None]
-    normal_feat = (residual - center[..., None]) * inv_std
-    gain_float = norm_gain.astype(jnp.float32)
-    pooled = jnp.mean(normal_feat * gain_float, axis=1).astype(jnp.bfloat16)
+    placed_stream = lax.dynamic_update_slice_in_dim(
+        jnp.zeros(partial_value.shape, jnp.float32),
+        stream.astype(jnp.float32),
+        t_index * feat_share,
+        2,
+    )
+    residual = lax.psum((partial_value + placed_stream).astype(jnp.bfloat16), "tensor").astype(
+        jnp.float32
+    )
+    center = jnp.mean(residual, axis=-1, keepdims=True)
+    offset = residual - center
+    variance = jnp.mean(offset * offset, axis=-1, keepdims=True)
+    inv_std = lax.rsqrt(variance + EPSILON)
+    normal_feat = offset * inv_std
+    pooled_full = jnp.mean(normal_feat * gain_full, axis=1)
+    pooled = lax.dynamic_slice_in_dim(pooled_full, t_index * feat_share, feat_share, 1).astype(
+        jnp.bfloat16
+    )
     embedded = lax.psum(jnp.dot(pooled, proj_weight, preferred_element_type=jnp.float32), "tensor")
     embed_norm = jnp.sqrt(jnp.sum(embedded * embedded, axis=-1, keepdims=True) + EPSILON)
     spectra = embedded / embed_norm
-    gathered = lax.all_gather(images, "dp", axis=0, tiled=True).astype(jnp.float32)
-    image_unit = gathered / jnp.sqrt(jnp.sum(gathered * gathered, axis=-1, keepdims=True) + EPSILON)
     logits = SCALE_LOGIT * jnp.dot(spectra, image_unit.T, precision=HIGH)
     own_start = lax.axis_index("dp") * seq_count
     columns = jnp.arange(logits.shape[1], dtype=jnp.int32)
@@ -101,20 +121,17 @@
     grad_pooled = lax.dot_general(
         grad_embed, proj_weight, (((1,), (1,)), ((), ())), preferred_element_type=jnp.float32
     )
-    grad_normal = jnp.broadcast_to(grad_pooled[:, None, :] / length, normal_feat.shape) * gain_float
-    mean_one, mean_two = lax.psum(
-        (jnp.sum(grad_normal, axis=-1), jnp.sum(grad_normal * normal_feat, axis=-1)), "tensor"
-    )
-    grad_resid = (
-        inv_std * (grad_normal - mean_one[..., None] / D - normal_feat * (mean_two[..., None] / D))
-    ).astype(jnp.bfloat16)
-    piece_rows = lax.all_gather(grad_resid, "tensor", axis=2, tiled=True)
+    grad_pooled_full = lax.all_gather(grad_pooled, "tensor", axis=1, tiled=True)
+    grad_normal = jnp.broadcast_to(
+        grad_pooled_full[:, None, :] / length, normal_feat.shape
+    ) * gain_full
+    mean_one = jnp.mean(grad_normal, axis=-1, keepdims=True)
+    mean_two = jnp.mean(grad_normal * normal_feat, axis=-1, keepdims=True)
+    piece_rows = (inv_std * (grad_normal - mean_one - normal_feat * mean_two)).astype(jnp.bfloat16)
     grad_heads = jnp.einsum(
         "blw,cw->blc", piece_rows, out_weight, preferred_element_type=jnp.float32
     )
-    update = jnp.einsum("blc,blw->cw", head_concat, piece_rows, preferred_element_type=jnp.float32)
-    grad_out = update
-    grad_heads, grad_out = (grad_heads, grad_out)
+    grad_out = jnp.einsum("blc,blw->cw", head_concat, piece_rows, preferred_element_type=jnp.float32)
     grad_heads = split_heads(grad_heads.astype(jnp.bfloat16), head_size)
     grad_probs = jnp.einsum(
         "bqhd,bkhd->bhqk", grad_heads, values_all, preferred_element_type=jnp.float32
@@ -149,24 +166,39 @@
     grad_query = jnp.einsum("bld,blc->dc", normed, grad_q, preferred_element_type=jnp.float32)
     grad_key = jnp.einsum("bld,blc->dc", normed, grad_k, preferred_element_type=jnp.float32)
     grad_value = jnp.einsum("bld,blc->dc", normed, grad_v, preferred_element_type=jnp.float32)
-    reduced = (
-        lax.psum_scatter(
-            grad_query.astype(jnp.bfloat16), "dp", scatter_dimension=0, tiled=True
-        ).astype(jnp.float32),
-        lax.psum_scatter(
-            grad_key.astype(jnp.bfloat16), "dp", scatter_dimension=0, tiled=True
-        ).astype(jnp.float32),
-        lax.psum_scatter(
-            grad_value.astype(jnp.bfloat16), "dp", scatter_dimension=0, tiled=True
-        ).astype(jnp.float32),
-        lax.psum_scatter(
-            grad_out.astype(jnp.bfloat16), "dp", scatter_dimension=1, tiled=True
-        ).astype(jnp.float32),
-        lax.psum_scatter(
-            grad_proj.astype(jnp.bfloat16), "dp", scatter_dimension=1, tiled=True
-        ).astype(jnp.float32),
-    )
-    return (mean_loss, grad_normed, reduced[0], reduced[1], reduced[2], reduced[3], reduced[4])
+    pieces = [
+        chunks_rows(grad_query.astype(jnp.bfloat16), dp_parts),
+        chunks_rows(grad_key.astype(jnp.bfloat16), dp_parts),
+        chunks_rows(grad_value.astype(jnp.bfloat16), dp_parts),
+        chunks_cols(grad_out.astype(jnp.bfloat16), dp_parts),
+        chunks_cols(grad_proj.astype(jnp.bfloat16), dp_parts),
+    ]
+    widths = [piece.shape[1] for piece in pieces]
+    joined = jnp.concatenate(pieces, axis=1)
+    total_width = joined.shape[1]
+    reduced = lax.psum_scatter(
+        joined.reshape(dp_parts * 8, total_width // 8), "dp", scatter_dimension=0, tiled=True
+    ).astype(jnp.float32).reshape(1, total_width)
+    outs = []
+    start = 0
+    for width in widths:
+        outs.append(reduced[0, start:start + width])
+        start += width
+    rows_q = D // dp_parts
+    grad_query_out = outs[0].reshape(rows_q, col_count)
+    grad_key_out = outs[1].reshape(rows_q, col_count)
+    grad_value_out = outs[2].reshape(rows_q, col_count)
+    grad_out_out = outs[3].reshape(grad_out.shape[0], grad_out.shape[1] // dp_parts)
+    grad_proj_out = outs[4].reshape(grad_proj.shape[0], grad_proj.shape[1] // dp_parts)
+    return (
+        mean_loss,
+        grad_normed,
+        grad_query_out,
+        grad_key_out,
+        grad_value_out,
+        grad_out_out,
+        grad_proj_out,
+    )
 
 
 def solution(mesh):

time: 982 us -> 603 us (0.61)
  waiting for transfers between devices: 665 us -> 255 us
  local copies, waits for them, and re-layouts: 14.2 us -> 43.2 us
    unnamed x11 -> x3, waiting for transfers between devices: 268 us -> 0.05 us
    all_gather x1 -> x0, waiting for transfers between devices: 73.9 us -> none  [local(): piece_rows = lax.all_gather(grad_resid, 'tensor', axis=2, tiled=True)]
    psum x3 -> x0, blocking collectives: 39.7 us -> none  [the longest x1 13.8 us: local(): variance = lax.psum(jnp.sum(offset * offset, axis=-1), 'tensor') / D]
    all_gather x0 -> x2, blocking collectives: none -> 35.7 us  [the longest x1 19.2 us: local(): grad_pooled_full = lax.all_gather(grad_pooled, 'tensor', axis=1, tiled=True)]
    reduce_scatter x1, waiting for transfers between devices: 82.3 us -> 53.2 us  [local(): lax.psum_scatter(back_input.astype(jnp.bfloat16), 'tensor', scatter_dimen...]
    reduce_scatter x2 -> x1, waiting for transfers between devices: 124 us -> 103 us  [local(): lax.psum_scatter(joined.reshape(dp_parts * 8, total_width // 8), 'dp', sc...]
    psum x1, waiting for transfers between devices: 117 us -> 98.8 us  [local(): lax.psum((partial_value + placed_stream).astype(jnp.bfloat16), 'tensor')]
    reshape x0 -> x6, local copies, waits for them, and re-layouts: none -> 14.5 us  [the longest x1 6.02 us: local(): joined.reshape(dp_parts * 8, total_width // 8)]
  transfers between devices with their start and end apart: 8 -> 3, of which waited for: 8 -> 3; matrix products, arithmetic and copies ran while one was open for 6% -> 5% of each run, Pallas kernels for 0% -> 0%
where the time goes in v1:
time: 603 us; the launch traced here: 592 us
  waiting for transfers between devices  255 us (42%)
  blocking collectives  177 us (29%)
  matrix products  77.7 us (13%)
  local copies, waits for them, and re-layouts  43.2 us (7%)
  other arithmetic  21.3 us (4%)
  between operations  18.3 us (3%)
    reduce_scatter x1, waiting for transfers between devices, local(): lax.psum_scatter(joined.reshape(dp_parts * 8, total_width // 8), 'dp', sc...  103 us
    psum x1, waiting for transfers between devices, local(): lax.psum((partial_value + placed_stream).astype(jnp.bfloat16), 'tensor')  98.8 us
    psum x1, blocking collectives, local(): lax.psum((jnp.sum(exp_logits, axis=0), local_loss), 'dp')  75.8 us
    reduce_scatter x1, waiting for transfers between devices, local(): lax.psum_scatter(back_input.astype(jnp.bfloat16), 'tensor', scatter_dimen...  53.2 us
    all_gather x1, blocking collectives, local(): lax.all_gather(images, 'dp', axis=0, tiled=True).astype(jnp.float32)  52.4 us
    all_gather x1, blocking collectives, local(): grad_pooled_full = lax.all_gather(grad_pooled, 'tensor', axis=1, tiled=True)  19.2 us
    all_gather x1, blocking collectives, local(): lax.all_gather(norm_gain, 'tensor', axis=0, tiled=True).astype(jnp.float32)  16.5 us
    psum x1, blocking collectives, local(): lax.psum(jnp.dot(pooled, proj_weight, preferred_element_type=jnp.float32)...  13.1 us
  transfers between devices with their start and end apart: 3, of which 3 were waited for; matrix products, arithmetic and copies ran while one was open for 5% of the time, Pallas kernels for 0%

profile of v1, /device:TPU:1, one launch (start us, length us, event | category | flops | bytes accessed | tf_op | source)
XLA Modules:
  0.0 592.3 jit_solution(5410974256325778971)
XLA Ops:
  7.2 4.5 fusion.52
  11.9 4.0 fusion.55
  16.7 2.8 fusion.130
  21.5 2.0 fusion.49
  23.7 4.7 fusion.58
  29.1 4.0 fusion.67
  33.1 2.2 add_dynamic-update-slice_fusion
  35.4 5.6 convert_element_type.104
  41.7 16.5 %all-gather = bf16[8,1,256]{2,1,0:T(2,128)(2,1)S(1)} all-gather(bf16[1,1,256]{2,1,0:T(2,128)(2,1)S(1)} %reshape.135), channel_id=1, replica_groups=mesh['dp'=32,'tensor'=8] {'tensor'}, dimensions={0}, use_global_device_ids=true | all-gather | bytes 4608 | tf_op jit(solution)/shard_map/all_gather | solution.py:55
  58.2 52.4 %all-gather.1 = bf16[32,2,1024]{2,1,0:T(2,128)(2,1)S(1)} all-gather(bf16[1,2,1024]{2,1,0:T(2,128)(2,1)S(1)} %bitcast.86), channel_id=1, replica_groups=mesh['dp'=32,'tensor'=8] {'dp'}, dimensions={0}, use_global_device_ids=true | all-gather | bytes 135168 | tf_op jit(solution)/shard_map/all_gather | solution.py:56
  110.8 98.8 %all-reduce.3.cloned.1.call-done = bf16[2,430,2048]{2,1,0:T(8,128)(2,1)} async-done(((bf16[2,430,2048]{2,1,0:T(8,128)(2,1)}), bf16[2,430,2048]{2,1,0:T(8,128)(2,1)}) %all-reduce.3.cloned.1.call-update) | async-done | bytes 3522576 | tf_op jit(solution)/shard_map/psum | solution.py:83
  209.5 2.7 convert_reduce_fusion
  212.6 1.1 fusion.10
  213.7 1.3 fusion.6
  215.2 13.1 %psum.29 = f32[2,1024]{1,0:T(2,128)S(1)} all-reduce(f32[2,1024]{1,0:T(2,128)S(1)} %fusion.115), channel_id=1, replica_groups=mesh['dp'=32,'tensor'=8] {'tensor'}, use_global_device_ids=true, to_apply=%region_6.0 | all-reduce | flops 2048 | bytes 16384 | tf_op jit(solution)/shard_map/psum | solution.py:95
  231.4 75.8 %all-reduce = (f32[]{:T(128)}, f32[64]{0:T(128)S(1)}) all-reduce(f32[]{:T(128)S(6)} %sub.64, f32[64]{0:T(128)S(1)} %get-tuple-element.34), channel_id=1, replica_groups=mesh['dp'=32,'tensor'=8] {'dp'}, use_global_device_ids=true, to_apply=%region_12.0 | all-reduce | flops 65 | bytes 520 | tf_op jit(solution)/shard_map/psum | solution.py:107
  308.8 19.2 %all_gather.11 = f32[2,2048]{1,0:T(2,128)S(1)} all-gather(f32[2,256]{1,0:T(2,128)S(1)} %fusion.118), channel_id=1, replica_groups=mesh['dp'=32,'tensor'=8] {'tensor'}, dimensions={1}, use_global_device_ids=true | all-gather | bytes 18432 | tf_op jit(solution)/shard_map/all_gather | solution.py:124
  328.1 3.0 multiply_reduce_fusion
  331.1 2.3 convolution_convert_fusion.2
  333.5 2.4 fusion.82
  335.9 7.3 %fusion.60 = bf16[2,430,2,128]{3,1,2,0:T(8,128)(2,1)} fusion(f32[2,2,430,430]{2,3,1,0:T(8,128)} %fusion.82, bf16[2,430,2,128]{3,2,1,0:T(2,128)(2,1)S(1)} %reshape.116, f32[2,2,430,430]{2,3,1,0:T(8,128)} %get-tuple-element.44, f32[2,2,430]{2,1,0:T(2,128)S(1)} %get-tuple-element.43), kind=kOutput, calls=%fused_computation.61 | convolution fusion | flops 194737104 | bytes 6804320 | tf_op jit(solution)/shard_map/bhqk,bqhd->bkhd/dot_general | solution.py:147
  343.2 6.9 %fusion.63 = bf16[2,430,2,128]{3,1,2,0:T(8,128)(2,1)S(1)} fusion(f32[2,2,430,430]{2,3,1,0:T(8,128)} %fusion.82, bf16[2,430,2,128]{3,2,1,0:T(2,128)(2,1)S(1)} %reshape.117, f32[2,2,430,430]{2,3,1,0:T(8,128)} %get-tuple-element.44, f32[2,2,430]{2,1,0:T(2,128)S(1)} %get-tuple-element.43), kind=kOutput, calls=%fused_computation.62 | convolution fusion | flops 194737104 | bytes 6804320 | tf_op jit(solution)/shard_map/bhqk,bkhd->bqhd/dot_general | solution.py:142
  350.1 5.1 fusion.59
  355.9 5.4 fusion.24
  361.3 4.0 fusion.72
  366.6 3.1 reshape.129
  369.7 4.5 fusion.21
  374.7 1.1 copy.90
  375.8 1.7 reshape.127
  377.5 1.4 copy.80
  379.9 1.5 copy.84
  381.9 1.1 constant_dynamic-update-slice_fusion.4
  383.0 1.4 copy.82
  384.7 2.5 fusion.69
  387.2 6.2 %add_convert_fusion = bf16[2,430,2048]{2,1,0:T(8,128)(2,1)} fusion(f32[2,430,2048]{2,1,0:T(8,128)} %fusion.72, f32[2,430,2048]{2,1,0:T(8,128)S(1)} %fusion.69, bf16[2,430,256]{2,1,0:T(8,128)(2,1)S(1)} %reshape.122, bf16[2048,256]{1,0:T(8,128)(2,1)S(1)} %copy-done.15), kind=kOutput, calls=%fused_computation.17 | convolution fusion | flops 907059200 | bytes 19101696 | tf_op jit(solution)/shard_map/blc,dc->bld/dot_general | solution.py:160
  394.5 4.4 fusion.23
  398.9 1.5 copy.86
  400.4 1.6 reshape.124
  402.0 4.6 fusion.22
  406.6 1.3 copy.88
  407.9 1.6 reshape.125
  409.5 1.0 constant_dynamic-update-slice_fusion.3
  410.5 1.0 constant_dynamic-update-slice_fusion.2
  411.6 1.1 constant_dynamic-update-slice_fusion.1
  413.5 6.0 %reshape.130 = bf16[256,9216]{1,0:T(8,128)(2,1)} reshape(bf16[32,73728]{1,0:T(8,128)(2,1)} %constant_dynamic-update-slice_fusion) | data formatting | bytes 9437184 | tf_op jit(solution)/shard_map/reshape | solution.py:180
  420.9 53.2 %reduce-scatter.3.cloned.1.call-done = bf16[2,430,256]{2,1,0:T(8,128)(2,1)} async-done(((bf16[2,430,2048]{2,1,0:T(8,128)(2,1)}), bf16[2,430,256]{2,1,0:T(8,128)(2,1)}) %reduce-scatter.3.cloned.1.call-update) | async-done | bytes 440336 | tf_op jit(solution)/shard_map/reduce_scatter | solution.py:163
  474.1 2.1 copy.93
  476.2 102.6 %reduce-scatter.5.cloned.1.call-done = bf16[8,9216]{1,0:T(8,128)(2,1)} async-done(((bf16[256,9216]{1,0:T(8,128)(2,1)}), bf16[8,9216]{1,0:T(8,128)(2,1)}) %reduce-scatter.5.cloned.1.call-update) | async-done | bytes 147472 | tf_op jit(solution)/shard_map/reduce_scatter | solution.py:179
  (92 shorter events, 20.2 us)
Async XLA Ops:
  7.2 21.9 %copy-start = (bf16[256,2048]{1,0:T(8,128)(2,1)S(1)}, bf16[256,2048]{1,0:T(8,128)(2,1)}, u32[]{:S(2)}) copy-start(bf16[256,2048]{1,0:T(8,128)(2,1)} %param.14) | copy-start | bytes 3145732
  7.2 202.4 %all-reduce.3.cloned.1.call-start = ((), (), s32[]{:S(2)}) async-start(), calls=%async_computation.2 | async-start | bytes 7077888 | tf_op jit(solution)/shard_map/psum | solution.py:83
  7.2 4.6 copy-start.13
  16.7 3.6 copy-start.5
  16.7 4.6 copy-start.4
  16.7 4.8 copy-start.14
  29.1 4.0 copy-start.10
  29.1 4.0 copy-start.17
  41.0 0.7 copy-start.19
  41.0 17.2 %copy-start.18 = (bf16[2,1024]{1,0:T(2,128)(2,1)S(1)}, bf16[2,1024]{1,0:T(2,128)(2,1)}, u32[]{:S(2)}) copy-start(bf16[2,1024]{1,0:T(2,128)(2,1)} %param.17) | copy-start | bytes 12292
  41.0 433.1 %reduce-scatter.3.cloned.1.call-start = ((), (), s32[]{:S(2)}) async-start(), calls=%async_computation.3 | async-start | bytes 3981312 | tf_op jit(solution)/shard_map/reduce_scatter | solution.py:163
  209.5 3.1 copy-start.2
  212.6 2.4 copy-start.16
  307.2 23.9 %copy-start.3 = (bf16[2,430,2048]{2,1,0:T(8,128)(2,1)S(1)}, bf16[2,430,2048]{2,1,0:T(8,128)(2,1)}, u32[]{:S(2)}) copy-start(bf16[2,430,2048]{2,1,0:T(8,128)(2,1)} %all-reduce.3.cloned.1.call-done) | copy-start | bytes 10567684
  355.2 6.0 %copy-start.12 = (bf16[2048,256]{1,0:T(8,128)(2,1)S(1)}, bf16[2048,256]{1,0:T(8,128)(2,1)}, u32[]{:S(2)}) copy-start(bf16[2048,256]{1,0:T(8,128)(2,1)} %param.11) | copy-start | bytes 3145732
  365.3 4.4 copy-start.11
  381.9 2.8 copy-start.6
  384.7 2.5 copy-start.8
  384.7 2.5 copy-start.15
  393.5 1.0 copy-start.7
  393.5 185.3 %reduce-scatter.5.cloned.1.call-start = ((), (), s32[]{:S(2)}) async-start(), calls=%async_computation.4 | async-start | bytes 4866048 | tf_op jit(solution)/shard_map/reduce_scatter | solution.py:179
  409.5 3.2 copy-start.9
  419.5 164.9 %copy-start.1 = (bf16[256,2048]{1,0:T(8,128)(2,1)S(1)}, bf16[256,2048]{1,0:T(8,128)(2,1)}, u32[]{:S(2)}) copy-start(bf16[256,2048]{1,0:T(8,128)(2,1)} %param.14) | copy-start | bytes 3145732
Sparse Core Ops, SparseCore 0:
  41.2 168.3 all-reduce.2
  393.6 80.4 reduce-scatter.2
  478.2 100.6 reduce-scatter.4

commit v2 on v1

--- a/solution.py
+++ b/solution.py
@@ -31,6 +31,51 @@
 def chunks_cols(grad, parts):
     rows, cols = grad.shape
     return grad.reshape(rows, parts, cols // parts).transpose(1, 0, 2).reshape(parts, -1)
+
+
+def xor_pairs(count, bit):
+    return [(i, i ^ bit) for i in range(count)]
+
+
+def tree_sum(value, axis, count):
+    bit = 1
+    while bit < count:
+        value = value + lax.ppermute(value, axis, xor_pairs(count, bit))
+        bit *= 2
+    return value
+
+
+def tree_gather(value, axis, count, dim):
+    index = lax.axis_index(axis)
+    bit = 1
+    while bit < count:
+        other = lax.ppermute(value, axis, xor_pairs(count, bit))
+        low = (index // bit) % 2 == 0
+        value = jnp.where(
+            low,
+            jnp.concatenate([value, other], dim),
+            jnp.concatenate([other, value], dim),
+        )
+        bit *= 2
+    return value
+
+
+def tree_scatter(buffer, axis, count):
+    index = lax.axis_index(axis)
+    total = None
+    bit = 1
+    step = 0
+    while bit < count:
+        rows = buffer.shape[0]
+        halves = buffer.reshape(rows // 2, 2, buffer.shape[1])
+        own = (index // bit) % 2
+        keep = lax.dynamic_index_in_dim(halves, own, axis=1, keepdims=False)
+        send = lax.dynamic_index_in_dim(halves, 1 - own, axis=1, keepdims=False)
+        received = lax.ppermute(send.astype(jnp.bfloat16), axis, xor_pairs(count, bit))
+        buffer = keep.astype(jnp.float32) + received.astype(jnp.float32)
+        bit *= 2
+        step += 1
+    return buffer
 
 
 def local(
@@ -51,9 +96,10 @@
     head_size = D // H
     scale_head = head_size ** (-0.5)
     dp_parts = lax.psum(1, "dp")
+    t_parts = lax.psum(1, "tensor")
     t_index = lax.axis_index("tensor")
-    gain_full = lax.all_gather(norm_gain, "tensor", axis=0, tiled=True).astype(jnp.float32)
-    gathered = lax.all_gather(images, "dp", axis=0, tiled=True).astype(jnp.float32)
+    gain_full = tree_gather(norm_gain, "tensor", t_parts, 0).astype(jnp.float32)
+    gathered = tree_gather(images, "dp", dp_parts, 0).astype(jnp.float32)
     image_unit = gathered / jnp.sqrt(jnp.sum(gathered * gathered, axis=-1, keepdims=True) + EPSILON)
 
     queries = split_heads(project(normed, query_weight), head_size)
@@ -92,7 +138,9 @@
     pooled = lax.dynamic_slice_in_dim(pooled_full, t_index * feat_share, feat_share, 1).astype(
         jnp.bfloat16
     )
-    embedded = lax.psum(jnp.dot(pooled, proj_weight, preferred_element_type=jnp.float32), "tensor")
+    embedded = tree_sum(
+        jnp.dot(pooled, proj_weight, preferred_element_type=jnp.float32), "tensor", t_parts
+    )
     embed_norm = jnp.sqrt(jnp.sum(embedded * embedded, axis=-1, keepdims=True) + EPSILON)
     spectra = embedded / embed_norm
     logits = SCALE_LOGIT * jnp.dot(spectra, image_unit.T, precision=HIGH)
@@ -104,7 +152,11 @@
     row_lse = jnp.log(jnp.sum(exp_logits, axis=1))
     diagonal = jnp.sum(logits * matches, axis=1)
     local_loss = 0.5 * jnp.sum(row_lse) - jnp.sum(diagonal)
-    col_total, loss_sum = lax.psum((jnp.sum(exp_logits, axis=0), local_loss), "dp")
+    loss_terms = tree_sum(
+        jnp.concatenate([jnp.sum(exp_logits, axis=0), local_loss[None]]), "dp", dp_parts
+    )
+    col_total = loss_terms[:-1]
+    loss_sum = loss_terms[-1]
     col_lse = jnp.log(col_total)
     mean_loss = (loss_sum + 0.5 * jnp.sum(col_lse)) / logits.shape[1]
     grad_logits = GRAD_SCALE * (
@@ -121,7 +173,7 @@
     grad_pooled = lax.dot_general(
         grad_embed, proj_weight, (((1,), (1,)), ((), ())), preferred_element_type=jnp.float32
     )
-    grad_pooled_full = lax.all_gather(grad_pooled, "tensor", axis=1, tiled=True)
+    grad_pooled_full = tree_gather(grad_pooled, "tensor", t_parts, 1)
     grad_normal = jnp.broadcast_to(
         grad_pooled_full[:, None, :] / length, normal_feat.shape
     ) * gain_full
@@ -174,11 +226,7 @@
         chunks_cols(grad_proj.astype(jnp.bfloat16), dp_parts),
     ]
     widths = [piece.shape[1] for piece in pieces]
-    joined = jnp.concatenate(pieces, axis=1)
-    total_width = joined.shape[1]
-    reduced = lax.psum_scatter(
-        joined.reshape(dp_parts * 8, total_width // 8), "dp", scatter_dimension=0, tiled=True
-    ).astype(jnp.float32).reshape(1, total_width)
+    reduced = tree_scatter(jnp.concatenate(pieces, axis=1), "dp", dp_parts)
     outs = []
     start = 0
     for width in widths:

time: 603 us -> 598 us (level)
  blocking collectives: 177 us -> 0 us
  waiting for transfers between devices: 255 us -> 319 us
  starting transfers between devices: 0.12 us -> 58.2 us
  local copies, waits for them, and re-layouts: 43.2 us -> 69 us
  other arithmetic: 21.3 us -> 43.1 us
    reduce_scatter x1 -> x0, waiting for transfers between devices: 103 us -> none  [local(): lax.psum_scatter(joined.reshape(dp_parts * 8, total_width // 8), 'dp', sc...]
    ppermute x0 -> x24, waiting for transfers between devices: none -> 99.6 us  [the longest x5 78.7 us: tree_scatter(): lax.ppermute(send.astype(jnp.bfloat16), axis, xor_pairs(count, bit))]
    psum x2 -> x0, blocking collectives: 88.9 us -> none  [the longest x1 75.8 us: local(): lax.psum((jnp.sum(exp_logits, axis=0), local_loss), 'dp')]
    all_gather x3 -> x0, blocking collectives: 88.1 us -> none  [the longest x1 52.4 us: local(): lax.all_gather(images, 'dp', axis=0, tiled=True).astype(jnp.float32)]
    ppermute x0 -> x24, starting transfers between devices: none -> 58.1 us  [the longest x11 21.7 us: tree_gather(): other = lax.ppermute(value, axis, xor_pairs(count, bit))]
    psum x1, waiting for transfers between devices: 98.8 us -> 144 us  [local(): lax.psum((partial_value + placed_stream).astype(jnp.bfloat16), 'tensor')]
    reduce_scatter x1, waiting for transfers between devices: 53.2 us -> 75.9 us  [local(): lax.psum_scatter(back_input.astype(jnp.bfloat16), 'tensor', scatter_dimen...]
    dynamic_slice x0 -> x1, other arithmetic: none -> 15.8 us  [tree_scatter(): send = lax.dynamic_index_in_dim(halves, 1 - own, axis=1, keepdims=False)]
  transfers between devices with their start and end apart: 3 -> 26, of which waited for: 3 -> 17; matrix products, arithmetic and copies ran while one was open for 5% -> 7% of each run, Pallas kernels for 0% -> 0%
where the time goes in v2:
time: 598 us; the launch traced here: 588 us
  waiting for transfers between devices  319 us (53%)
  matrix products  80.2 us (13%)
  local copies, waits for them, and re-layouts  69 us (12%)
  starting transfers between devices  58.2 us (10%)
  other arithmetic  43.1 us (7%)
  between operations  18.9 us (3%)
    psum x1, waiting for transfers between devices, local(): lax.psum((partial_value + placed_stream).astype(jnp.bfloat16), 'tensor')  144 us
    ppermute x5, waiting for transfers between devices, tree_scatter(): lax.ppermute(send.astype(jnp.bfloat16), axis, xor_pairs(count, bit))  78.7 us
    reduce_scatter x1, waiting for transfers between devices, local(): lax.psum_scatter(back_input.astype(jnp.bfloat16), 'tensor', scatter_dimen...  75.9 us
    ppermute x11, starting transfers between devices, tree_gather(): other = lax.ppermute(value, axis, xor_pairs(count, bit))  21.7 us
    ppermute x5, starting transfers between devices, tree_scatter(): lax.ppermute(send.astype(jnp.bfloat16), axis, xor_pairs(count, bit))  19 us
    unnamed x71, local copies, waits for them, and re-layouts  18.8 us
    ppermute x8, starting transfers between devices, tree_sum(): value = value + lax.ppermute(value, axis, xor_pairs(count, bit))  17.4 us
    dynamic_slice x1, other arithmetic, tree_scatter(): send = lax.dynamic_index_in_dim(halves, 1 - own, axis=1, keepdims=False)  15.8 us
  transfers between devices with their start and end apart: 26, of which 17 were waited for; matrix products, arithmetic and copies ran while one was open for 7% of the time, Pallas kernels for 0%

profile of v2, /device:TPU:1, one launch (start us, length us, event | category | flops | bytes accessed | tf_op | source)
XLA Modules:
  0.0 588.5 jit_solution(12534343313260771682)
XLA Ops:
  7.2 4.5 fusion.52
  11.9 4.2 fusion.55
  16.9 2.9 fusion.138
  23.9 4.8 fusion.58
  31.2 2.4 convert_element_type.151
  34.3 2.5 collective-permute-start
  38.6 3.1 collective-permute-start.7
  43.1 5.1 collective-permute-start.8
  48.2 3.0 collective-permute-start.2
  54.5 2.8 collective-permute-start.10
  57.3 143.6 %all-reduce.2.cloned.1.call-done = bf16[2,430,2048]{2,1,0:T(8,128)(2,1)} async-done(((bf16[2,430,2048]{2,1,0:T(8,128)(2,1)}), bf16[2,430,2048]{2,1,0:T(8,128)(2,1)}) %all-reduce.2.cloned.1.call-update) | async-done | bytes 3522576 | tf_op jit(solution)/shard_map/psum | solution.py:129
  200.9 2.7 convert_reduce_fusion
  206.7 2.4 collective-permute-done.3
  218.7 4.7 collective-permute-start.11
  227.6 4.6 collective-permute-start.13
  236.4 2.7 collective-permute-start.15
  241.6 2.8 collective-permute-done.16
  244.4 2.4 collective-permute-done.17
  251.7 2.7 concatenate.138
  254.4 3.2 multiply_reduce_fusion
  257.6 2.3 convolution_convert_fusion.2
  260.1 2.5 fusion.84
  262.6 7.4 %fusion.60 = bf16[2,430,2,128]{3,1,2,0:T(8,128)(2,1)} fusion(f32[2,2,430,430]{2,3,1,0:T(8,128)} %fusion.84, bf16[2,430,2,128]{3,2,1,0:T(2,128)(2,1)S(1)} %copy-done.13, f32[2,2,430,430]{2,3,1,0:T(8,128)} %get-tuple-element.46, f32[2,2,430]{2,1,0:T(2,128)S(1)} %get-tuple-element.45), kind=kOutput, calls=%fused_computation.66 | convolution fusion | flops 194737104 | bytes 6804320 | tf_op jit(solution)/shard_map/bhqk,bqhd->bkhd/dot_general | solution.py:199
  270.0 7.6 %fusion.63 = bf16[2,430,2,128]{3,1,2,0:T(8,128)(2,1)} fusion(f32[2,2,430,430]{2,3,1,0:T(8,128)} %fusion.84, bf16[2,430,2,128]{3,2,1,0:T(2,128)(2,1)S(1)} %copy-done.15, f32[2,2,430,430]{2,3,1,0:T(8,128)} %get-tuple-element.46, f32[2,2,430]{2,1,0:T(2,128)S(1)} %get-tuple-element.45), kind=kOutput, calls=%fused_computation.67 | convolution fusion | flops 194737104 | bytes 6804320 | tf_op jit(solution)/shard_map/bhqk,bkhd->bqhd/dot_general | solution.py:194
  277.6 5.2 fusion.59
  282.8 4.4 fusion.21
  292.2 4.6 fusion.23
  301.9 4.6 fusion.24
  313.3 4.6 fusion.22
  327.4 15.8 %constant_dynamic-slice_fusion.5 = (bf16[16,1,73728]{2,1,0:T(2,128)(2,1)S(1)}, f32[16,1,73728]{2,1,0:T(1,128)}) fusion(bf16[16,2,73728]{2,1,0:T(2,128)(2,1)} %constant_dynamic-update-slice_fusion, s32[]{:T(128)S(6)} %select_n.259, s32[]{:T(128)S(6)} %select_n.258), kind=kLoop, calls=%fused_computation.140 | loop fusion | flops 1179648 | bytes 11796488 | tf_op jit(solution)/shard_map/jit(dynamic_index_in_dim)/dynamic_slice | solution.py:73
  343.3 2.6 copy.157
  345.9 7.5 %collective-permute-start.19 = (bf16[16,73728]{1,0:T(8,128)(2,1)S(1)}, bf16[16,73728]{1,0:T(8,128)(2,1)}, u32[]{:S(2)}, u32[]{:S(2)}) collective-permute-start(bf16[16,73728]{1,0:T(8,128)(2,1)S(1)} %bitcast.97), channel_id=1, source_target_pairs={{0,8},{8,0},{16,24},{24,16},{32,40},{40,32},{48,56},{56,48},{64,72... | collective-permute-start | bytes 7077896 | tf_op jit(solution)/shard_map/ppermute | solution.py:74
  355.3 5.4 fusion.70
  360.7 4.1 fusion.73
  364.8 6.7 %bitcast_add_fusion = f32[16,73728]{1,0:T(8,128)} fusion(f32[16,1,73728]{2,1,0:T(1,128)S(1)} %bitcast.95, bf16[16,73728]{1,0:T(8,128)(2,1)} %collective-permute-done.19), kind=kLoop, calls=%fused_computation.18 | loop fusion | flops 2359296 | bytes 11796480 | tf_op jit(solution)/shard_map/add | solution.py:75
  371.4 5.9 %reshape.228 = f32[8,2,73728]{2,1,0:T(2,128)} reshape(f32[16,73728]{1,0:T(8,128)} %bitcast_add_fusion) | data formatting | bytes 9437184 | tf_op jit(solution)/shard_map/reshape | solution.py:70
  377.4 4.6 constant_dynamic-slice_fusion.3
  383.3 2.6 collective-permute-start.20
  385.9 2.4 constant_dynamic-slice_fusion.4
  388.3 48.9 %collective-permute-done.20 = bf16[8,73728]{1,0:T(8,128)(2,1)S(1)} collective-permute-done((bf16[8,73728]{1,0:T(8,128)(2,1)S(1)}, bf16[8,73728]{1,0:T(8,128)(2,1)S(1)}, u32[]{:S(2)}, u32[]{:S(2)}) %collective-permute-start.20) | collective-permute-done | bytes 1179680 | tf_op jit(solution)/shard_map/ppermute | solution.py:74
  437.2 2.8 bitcast_add_fusion.1
  440.0 3.1 reshape.229
  444.9 4.9 collective-permute-start.21
  451.0 24.8 %collective-permute-done.21 = bf16[4,73728]{1,0:T(4,128)(2,1)S(1)} collective-permute-done((bf16[4,73728]{1,0:T(4,128)(2,1)S(1)}, bf16[4,73728]{1,0:T(4,128)(2,1)S(1)}, u32[]{:S(2)}, u32[]{:S(2)}) %collective-permute-start.21) | collective-permute-done | bytes 589856 | tf_op jit(solution)/shard_map/ppermute | solution.py:74
  480.6 4.9 collective-permute-done.22
  486.4 2.8 collective-permute-start.23
  489.2 8.1 %add_convert_fusion = bf16[2,430,2048]{2,1,0:T(8,128)(2,1)} fusion(f32[2,430,2048]{2,1,0:T(8,128)} %fusion.73, f32[2,430,2048]{2,1,0:T(8,128)} %fusion.70, bf16[2,430,256]{2,1,0:T(8,128)(2,1)S(1)} %copy-done.7, bf16[2048,256]{1,0:T(8,128)(2,1)S(1)} %copy-done.23), kind=kOutput, calls=%fused_computation.17 | convolution fusion | flops 907059200 | bytes 19101696 | tf_op jit(solution)/shard_map/blc,dc->bld/dot_general | solution.py:212
  502.1 75.9 %reduce-scatter.2.cloned.1.call-done = bf16[2,430,256]{2,1,0:T(8,128)(2,1)} async-done(((bf16[2,430,2048]{2,1,0:T(8,128)(2,1)}), bf16[2,430,256]{2,1,0:T(8,128)(2,1)}) %reduce-scatter.2.cloned.1.call-update) | async-done | bytes 440336 | tf_op jit(solution)/shard_map/reduce_scatter | solution.py:215
  (185 shorter events, 85.8 us)
Async XLA Ops:
  7.2 22.3 %copy-start = (bf16[256,2048]{1,0:T(8,128)(2,1)S(1)}, bf16[256,2048]{1,0:T(8,128)(2,1)}, u32[]{:S(2)}) copy-start(bf16[256,2048]{1,0:T(8,128)(2,1)} %param.14) | copy-start | bytes 3145732
  7.2 193.7 %all-reduce.2.cloned.1.call-start = ((), (), s32[]{:S(2)}) async-start(), calls=%async_computation.1 | async-start | bytes 7077888 | tf_op jit(solution)/shard_map/psum | solution.py:129
  7.2 4.6 copy-start.20
  11.9 4.4 copy-start.12
  16.2 3.5 copy-start.14
  16.9 3.6 copy-start.6
  16.9 4.6 copy-start.4
  16.9 4.8 copy-start.22
  23.9 4.9 copy-start.16
  33.7 544.3 %reduce-scatter.2.cloned.1.call-start = ((), (), s32[]{:S(2)}) async-start(), calls=%async_computation.2 | async-start | bytes 3981312 | tf_op jit(solution)/shard_map/reduce_scatter | solution.py:215
  34.3 7.4 %collective-permute-start = (bf16[256]{0:T(256)(128)(2,1)S(1)}, bf16[256]{0:T(256)(128)(2,1)S(1)}, u32[]{:S(2)}, u32[]{:S(2)}) collective-permute-start(bf16[256]{0:T(256)(128)(2,1)S(1)} %copy-done.27), channel_id=1, source_target_pairs={{0,1},{1,0},{2,3},{3,2},{4,5},{5,4},{6,7},{7,6},{8,9},{9,8},{10,11... | collective-permute-start | bytes 1544 | tf_op jit(solution)/shard_map/ppermute | solution.py:52
  36.8 1.8 collective-permute-start.6
  38.6 4.5 collective-permute-start.7
  41.6 6.5 %collective-permute-start.1 = (bf16[512]{0:T(512)(128)(2,1)S(1)}, bf16[512]{0:T(512)(128)(2,1)S(1)}, u32[]{:S(2)}, u32[]{:S(2)}) collective-permute-start(bf16[512]{0:T(512)(128)(2,1)S(1)} %maximum_select_fusion.10), channel_id=1, source_target_pairs={{0,2},{1,3},{2,0},{3,1},{4,6},{5,7},{6,4},{7,5},{8,10},{9,11},{10,... | collective-permute-start | bytes 3080 | tf_op jit(solution)/shard_map/ppermute | solution.py:52
  43.1 8.1 %collective-permute-start.8 = (bf16[8,1024]{1,0:T(8,128)(2,1)S(1)}, bf16[8,1024]{1,0:T(8,128)(2,1)S(1)}, u32[]{:S(2)}, u32[]{:S(2)}) collective-permute-start(bf16[8,1024]{1,0:T(8,128)(2,1)S(1)} %maximum_select_fusion.3), channel_id=1, source_target_pairs={{0,32},{8,40},{16,48},{24,56},{32,0},{40,8},{48,16},{56,24},{64,96... | collective-permute-start | bytes 49160 | tf_op jit(solution)/shard_map/ppermute | solution.py:52
  48.2 4.3 collective-permute-start.2
  51.2 3.3 collective-permute-start.9
  54.5 154.8 %collective-permute-start.10 = (bf16[32,1024]{1,0:T(8,128)(2,1)S(1)}, bf16[32,1024]{1,0:T(8,128)(2,1)S(1)}, u32[]{:S(2)}, u32[]{:S(2)}) collective-permute-start(bf16[32,1024]{1,0:T(8,128)(2,1)S(1)} %maximum_select_fusion.1), channel_id=1, source_target_pairs={{0,128},{8,136},{16,144},{24,152},{32,160},{40,168},{48,176},{56,1... | collective-permute-start | bytes 196616 | tf_op jit(solution)/shard_map/ppermute | solution.py:52
  206.6 2.5 collective-permute-start.3
  209.1 2.5 collective-permute-start.4
  211.6 4.0 collective-permute-start.5
  218.7 5.5 collective-permute-start.11
  224.3 3.3 collective-permute-start.12
  227.6 6.3 %collective-permute-start.13 = (f32[65]{0:T(128)S(1)}, f32[65]{0:T(128)S(1)}, u32[]{:S(2)}, u32[]{:S(2)}) collective-permute-start(f32[65]{0:T(128)S(1)} %add.206), channel_id=1, source_target_pairs={{0,32},{8,40},{16,48},{24,56},{32,0},{40,8},{48,16},{56,24},{64,96... | collective-permute-start | bytes 788 | tf_op jit(solution)/shard_map/ppermute | solution.py:43
  233.9 2.4 collective-permute-start.14
  236.4 3.9 collective-permute-start.15
  241.6 2.8 collective-permute-start.16
  244.4 2.5 collective-permute-start.17
  246.8 7.5 %collective-permute-start.18 = (f32[2,1024]{1,0:T(2,128)S(1)}, f32[2,1024]{1,0:T(2,128)S(1)}, u32[]{:S(2)}, u32[]{:S(2)}) collective-permute-start(f32[2,1024]{1,0:T(2,128)S(1)} %maximum_select_fusion.6), channel_id=1, source_target_pairs={{0,4},{1,5},{2,6},{3,7},{4,0},{5,1},{6,2},{7,3},{8,12},{9,13},{10,... | collective-permute-start | bytes 24584 | tf_op jit(solution)/shard_map/ppermute | solution.py:52
  254.4 3.2 copy-start.3
  262.6 7.4 %copy-start.15 = (bf16[2,430,2,128]{3,2,1,0:T(2,128)(2,1)S(1)}, bf16[2,430,2,128]{3,2,1,0:T(2,128)(2,1)}, u32[]{:S(2)}) copy-start(bf16[2,430,2,128]{3,2,1,0:T(2,128)(2,1)} %copy-done.14) | copy-start | bytes 1320964
  277.6 5.2 copy-start.19
  292.2 4.6 copy-start.8
  320.9 5.3 copy-start.11
  343.3 12.0 %copy-start.9 = (bf16[2,430,256]{2,1,0:T(8,128)(2,1)S(1)}, bf16[2,430,256]{2,1,0:T(8,128)(2,1)}, u32[]{:S(2)}) copy-start(bf16[2,430,256]{2,1,0:T(8,128)(2,1)} %copy-done.8) | copy-start | bytes 1320964
  345.9 18.9 %collective-permute-start.19 = (bf16[16,73728]{1,0:T(8,128)(2,1)S(1)}, bf16[16,73728]{1,0:T(8,128)(2,1)}, u32[]{:S(2)}, u32[]{:S(2)}) collective-permute-start(bf16[16,73728]{1,0:T(8,128)(2,1)S(1)} %bitcast.97), channel_id=1, source_target_pairs={{0,8},{8,0},{16,24},{24,16},{32,40},{40,32},{48,56},{56,48},{64,72... | collective-permute-start | bytes 7077896 | tf_op jit(solution)/shard_map/ppermute | solution.py:74
  355.3 5.4 copy-start.10
  355.3 5.4 copy-start.21
  355.3 9.5 %slice-start = ((s8[4718592]{0:T(1024)(128)(4,1)}), s8[4194304]{0:T(1024)(128)(4,1)S(1)}, s32[]{:S(2)}) async-start(s8[4718592]{0:T(1024)(128)(4,1)} %bitcast.94), calls=%async_computation.3 | async-start | bytes 8388608
  360.7 4.1 slice-start.1
  377.4 8.5 %copy-start.5 = (f32[8,2,73728]{2,1,0:T(2,128)S(1)}, f32[8,2,73728]{2,1,0:T(2,128)}, u32[]{:S(2)}) copy-start(f32[8,2,73728]{2,1,0:T(2,128)} %reshape.228) | copy-start | bytes 14155780
  383.3 53.9 %collective-permute-start.20 = (bf16[8,73728]{1,0:T(8,128)(2,1)S(1)}, bf16[8,73728]{1,0:T(8,128)(2,1)S(1)}, u32[]{:S(2)}, u32[]{:S(2)}) collective-permute-start(bf16[8,73728]{1,0:T(8,128)(2,1)S(1)} %bitcast.99), channel_id=1, source_target_pairs={{0,16},{8,24},{16,0},{24,8},{32,48},{40,56},{48,32},{56,40},{64,80... | collective-permute-start | bytes 3538952 | tf_op jit(solution)/shard_map/ppermute | solution.py:74
  444.9 31.0 %collective-permute-start.21 = (bf16[4,73728]{1,0:T(4,128)(2,1)S(1)}, bf16[4,73728]{1,0:T(4,128)(2,1)S(1)}, u32[]{:S(2)}, u32[]{:S(2)}) collective-permute-start(bf16[4,73728]{1,0:T(4,128)(2,1)S(1)} %bitcast.100), channel_id=1, source_target_pairs={{0,32},{8,40},{16,48},{24,56},{32,0},{40,8},{48,16},{56,24},{64,96... | collective-permute-start | bytes 1769480 | tf_op jit(solution)/shard_map/ppermute | solution.py:74
  477.7 11.5 %copy-start.7 = (bf16[2,430,256]{2,1,0:T(8,128)(2,1)S(1)}, bf16[2,430,256]{2,1,0:T(8,128)(2,1)}, u32[]{:S(2)}) copy-start(bf16[2,430,256]{2,1,0:T(8,128)(2,1)} %reshape.225) | copy-start | bytes 1320964
  477.7 11.5 %copy-start.23 = (bf16[2048,256]{1,0:T(8,128)(2,1)S(1)}, bf16[2048,256]{1,0:T(8,128)(2,1)}, u32[]{:S(2)}) copy-start(bf16[2048,256]{1,0:T(8,128)(2,1)} %param.13) | copy-start | bytes 3145732
  478.7 6.8 %collective-permute-start.22 = (bf16[2,73728]{1,0:T(2,128)(2,1)S(1)}, bf16[2,73728]{1,0:T(2,128)(2,1)S(1)}, u32[]{:S(2)}, u32[]{:S(2)}) collective-permute-start(bf16[2,73728]{1,0:T(2,128)(2,1)S(1)} %bitcast.101), channel_id=1, source_target_pairs={{0,64},{8,72},{16,80},{24,88},{32,96},{40,104},{48,112},{56,120},{... | collective-permute-start | bytes 884744 | tf_op jit(solution)/shard_map/ppermute | solution.py:74
  486.4 10.9 %collective-permute-start.23 = (bf16[1,73728]{1,0:T(2,128)(2,1)S(1)}, bf16[1,73728]{1,0:T(2,128)(2,1)S(1)}, u32[]{:S(2)}, u32[]{:S(2)}) collective-permute-start(bf16[1,73728]{1,0:T(2,128)(2,1)S(1)} %dynamic-slice_convert_fusion.2), channel_id=1, source_target_pairs={{0,128},{8,136},{16,144},{24,152},{32,160},{40,168},{48,176},{56,1... | collective-permute-start | bytes 442376 | tf_op jit(solution)/shard_map/ppermute | solution.py:74
  489.2 90.9 %copy-start.1 = (bf16[256,2048]{1,0:T(8,128)(2,1)S(1)}, bf16[256,2048]{1,0:T(8,128)(2,1)}, u32[]{:S(2)}) copy-start(bf16[256,2048]{1,0:T(8,128)(2,1)} %param.14) | copy-start | bytes 3145732
  (8 other events, 16.7 us)
Sparse Core Ops, SparseCore 0:
  33.8 167.0 all-reduce.1
  497.4 80.4 reduce-scatter.1
